TPU v7x, 256 devices: a whole 4x4x8 slice. The times are simulated.
256 devices in a mesh: tm: 16 (over z, core), head: 16 (over y, x).
Axes of the slice: x: 4, y: 4, z: 8, core: 2. Of those that a mesh axis runs over, the one named last changes fastest.
Arguments:
- frames: bfloat16 [8192, 2048], P(('tm', 'head')), may hold values from -6 to 6
- log_decay: float32 [8192, 16], P('tm', 'head'), may hold values from -2 to 0, as said below
- w_query: bfloat16 [2048, 2048], P('tm', 'head'), may hold values from -0.125 to 0.125
- w_key: bfloat16 [2048, 2048], P('tm', 'head'), may hold values from -0.125 to 0.125
- w_value: bfloat16 [2048, 2048], P('tm', 'head'), may hold values from -0.125 to 0.125
- w_gate: bfloat16 [2048, 2048], P('tm', 'head'), may hold values from -0.125 to 0.125
- w_out: bfloat16 [2048, 2048], P('head', 'tm'), may hold values from -0.125 to 0.125
Outputs:
- mixed: bfloat16 [8192, 2048], P(('tm', 'head'))
Inputs may be any that keep to these rules, and one draw needn't show every extreme that they name: `log_decay`: strictly negative.
All inputs are finite; a program needn't handle non-finite values.
Results may differ from a plain program's by a relative error of at most 0.015.
Values may be sent and summed in bfloat16 or wider, within the bound.
No kernel may reach another device: no remote copies, remote signals or barrier semaphores. Data moves between devices by JAX's collectives and lax.ppermute only.
A program may use at most 64 MiB of HBM per device.

v0:
```python
import jax
import jax.numpy as jnp
from jax import lax
from jax.sharding import PartitionSpec as P

HEAD_DIM = 128
BLOCK = 512
PAD_ROWS = 8


def prior_state(local_final, log_total, axis):
    heads_here = local_final.shape[0]
    extra = jnp.broadcast_to(log_total[:, None, None], (heads_here, PAD_ROWS, HEAD_DIM))
    packed = jnp.concatenate([local_final, extra], axis=1)
    gathered = lax.all_gather(packed, axis)
    finals = gathered[:, :, :HEAD_DIM, :]
    totals = gathered[:, :, HEAD_DIM, 0]
    count = gathered.shape[0]
    mine = lax.axis_index(axis)
    order = jnp.arange(count, dtype=jnp.int32)
    between = (order[:, None] < order[None, :]) & (order[None, :] < mine)
    exponent = jnp.sum(jnp.where(between[:, :, None], totals[None, :, :], 0.0), axis=1)
    weight = jnp.where((order < mine)[:, None], jnp.exp(exponent), 0.0)
    return jnp.sum(weight[:, :, None, None] * finals, axis=0)


def shards(frames, log_decay, w_query, w_key, w_value, w_gate, w_out):
    head_width = w_query.shape[1]
    joined = lax.all_gather(
        jnp.concatenate([w_query, w_key, w_value, w_gate], axis=1), "tm", axis=0, tiled=True
    )
    projected = jnp.dot(
        lax.all_gather(frames, "head", axis=0, tiled=True),
        joined,
        preferred_element_type=jnp.float32,
    )
    local_len = projected.shape[0]
    heads_here = head_width // HEAD_DIM
    block_count = local_len // BLOCK
    query_blocks = (
        projected[:, :head_width]
        .astype(jnp.bfloat16)
        .reshape(block_count, BLOCK, heads_here, HEAD_DIM)
    )
    key_blocks = (
        projected[:, head_width : 2 * head_width]
        .astype(jnp.bfloat16)
        .reshape(block_count, BLOCK, heads_here, HEAD_DIM)
    )
    value_blocks = (
        projected[:, 2 * head_width : 3 * head_width]
        .astype(jnp.bfloat16)
        .reshape(block_count, BLOCK, heads_here, HEAD_DIM)
    )
    gate_all = projected[:, 3 * head_width :]
    running_blocks = jnp.cumsum(log_decay.reshape(block_count, BLOCK, heads_here), axis=1)
    slice_ordinal = jnp.arange(BLOCK, dtype=jnp.int32)
    causal = slice_ordinal[:, None] >= slice_ordinal[None, :]

    def local_step(carry_state, inputs):
        query_block, key_block, value_block, running = inputs
        gaps = running.T[:, :, None] - running.T[:, None, :]
        decay = jnp.exp(jnp.where(causal[None], gaps, -jnp.inf))
        scores = jnp.einsum(
            "thd,shd->hts", query_block, key_block, preferred_element_type=jnp.float32
        )
        weights = (scores * decay).astype(jnp.bfloat16)
        intra = jnp.einsum("hts,shd->thd", weights, value_block, preferred_element_type=jnp.float32)
        scaled = (
            key_block.astype(jnp.float32) * jnp.exp(running[-1][None, :] - running)[:, :, None]
        ).astype(jnp.bfloat16)
        update = jnp.einsum("shd,she->hde", scaled, value_block, preferred_element_type=jnp.float32)
        next_state = jnp.exp(running[-1])[:, None, None] * carry_state + update
        return (next_state, (intra, carry_state))

    zero_state = jnp.zeros((heads_here, HEAD_DIM, HEAD_DIM), jnp.float32)
    local_final, (intra_all, local_starts) = lax.scan(
        local_step, zero_state, (query_blocks, key_blocks, value_blocks, running_blocks)
    )
    prior = prior_state(local_final, jnp.sum(log_decay, axis=0), "tm")
    block_logs = running_blocks[:, -1, :]
    before = jnp.cumsum(block_logs, axis=0) - block_logs
    start_states = jnp.exp(before)[:, :, None, None] * prior[None] + local_starts
    lifted = query_blocks.astype(jnp.float32) * jnp.exp(running_blocks)[..., None]
    inter = jnp.einsum("cthd,chde->cthe", lifted, start_states, precision=lax.Precision.HIGHEST)
    retained = (intra_all + inter).reshape(local_len, heads_here, HEAD_DIM)
    center = jnp.mean(retained, axis=-1, keepdims=True)
    spread = jnp.mean((retained - center) ** 2, axis=-1, keepdims=True)
    normed = (retained - center) / jnp.sqrt(spread + 1e-05)
    gated = (
        (jax.nn.silu(gate_all.reshape(local_len, heads_here, HEAD_DIM)) * normed)
        .astype(jnp.bfloat16)
        .reshape(local_len, head_width)
    )
    owned = lax.all_to_all(gated, "head", split_axis=0, concat_axis=1, tiled=True)
    rows_out = lax.all_gather(w_out, "tm", axis=1, tiled=True)
    return jnp.dot(
        owned,
        lax.all_gather(rows_out, "head", axis=0, tiled=True),
        preferred_element_type=jnp.float32,
    ).astype(jnp.bfloat16)


def solution(mesh):
    return jax.shard_map(
        shards,
        mesh=mesh,
        in_specs=(
            P(("tm", "head"), None),
            P("tm", "head"),
            P("tm", "head"),
            P("tm", "head"),
            P("tm", "head"),
            P("tm", "head"),
            P("head", "tm"),
        ),
        out_specs=P(("tm", "head"), None),
        check_vma=False,
    )
```

profile of v0, /device:TPU:1, one launch (start us, length us, event | category | flops | bytes accessed | tf_op | source)
XLA Modules:
  0.0 235.8 jit_solution(7422585032205424245)
XLA Ops:
  6.5 0.0 all-gather.8.cloned.1.call-start
  6.5 0.7 all-gather.8.cloned.1.call-update
  7.3 0.0 all-gather.6.cloned.1.call-start
  7.3 1.5 pad_maximum_fusion
  8.8 0.0 all-gather.6.cloned.1.call-update
  8.8 0.0 all-gather.12.cloned.1.call-start
  8.9 1.3 reduce_sum.45
  10.2 1.0 reduce-window.6
  11.1 0.7 slice.51
  11.8 0.2 slice_reduce_fusion.1
  12.0 0.2 reduce-window.9
  12.2 0.1 broadcast.153
  12.2 0.6 slice.52
  14.2 0.1 subtract_exponential_fusion
  14.3 0.0 copy-start
  14.3 48.5 %all-gather.8.cloned.1.call-done = bf16[512,2048]{1,0:T(8,128)(2,1)} async-done(((bf16[32,2048]{1,0:T(8,128)(2,1)}), bf16[512,2048]{1,0:T(8,128)(2,1)}) %all-gather.8.cloned.1.call-update) | async-done | bytes 2097168 | tf_op jit(solution)/shard_map/all_gather | solution.py:33
  62.7 42.3 %all-gather.6.cloned.1.call-done = bf16[2048,512]{1,0:T(8,128)(2,1)} async-done(((bf16[128,512]{1,0:T(8,128)(2,1)}), bf16[2048,512]{1,0:T(8,128)(2,1)}) %all-gather.6.cloned.1.call-update) | async-done | bytes 2097168 | tf_op jit(solution)/shard_map/all_gather | solution.py:29
  105.0 3.5 %fusion.35 = (bf16[512,512]{1,0:T(8,128)(2,1)S(1)}, f32[512,512]{1,0:T(8,128)S(1)}) fusion(bf16[512,2048]{1,0:T(8,128)(2,1)} %all-gather.8.cloned.1.call-done, bf16[2048,512]{1,0:T(8,128)(2,1)} %all-gather.6.cloned.1.call-done), kind=kOutput, calls=%fused_computation.55 | convolution fusion | flops 1074003968 | bytes 5767168 | tf_op jit(solution)/shard_map/dot_general | solution.py:32
  108.5 0.3 fusion.4
  108.8 1.3 concatenate.7
  110.1 0.0 all-gather.12.cloned.1.call-update
  110.1 0.0 all-gather.10.cloned.1.call-start
  110.1 0.0 copy-done
  110.1 19.1 %all_gather.22 = bf16[128,2048]{1,0:T(8,128)(2,1)} all-gather(bf16[128,128]{1,0:T(8,128)(2,1)S(1)} %copy-done), channel_id=1, replica_groups=mesh['tm'=16,'head'=16] {'tm'}, dimensions={1}, use_global_device_ids=true | all-gather | bytes 557056 | tf_op jit(solution)/shard_map/all_gather | solution.py:96
  129.2 0.0 all-gather.10.cloned.1.call-update
  129.2 0.6 slice.49
  129.9 0.6 slice.50
  131.9 0.5 fusion.2
  132.4 14.9 %all-gather.12.cloned.1.call-done = f32[16,136,128]{2,1,0:T(8,128)} async-done(((f32[1,136,128]{2,1,0:T(8,128)}), f32[16,136,128]{2,1,0:T(8,128)}) %all-gather.12.cloned.1.call-update) | async-done | bytes 1114128 | tf_op jit(solution)/shard_map/all_gather | solution.py:15
  147.3 1.0 slice_reduce_fusion
  148.4 0.1 select_reduce_fusion
  148.5 1.4 fusion.5
  149.9 0.5 fusion.36
  150.4 0.2 fusion.13
  150.7 0.2 fusion.16
  150.9 13.2 %all_to_all.19 = bf16[16,32,128]{2,1,0:T(8,128)(2,1)S(1)} all-to-all(bf16[16,32,128]{2,1,0:T(8,128)(2,1)S(1)} %bitcast.62), channel_id=1, replica_groups=mesh['tm'=16,'head'=16] {'head'}, dimensions={0} | all-to-all | bytes 262144 | tf_op jit(solution)/shard_map/all_to_all | solution.py:95
  164.0 59.6 %all-gather.10.cloned.1.call-done = bf16[2048,2048]{1,0:T(8,128)(2,1)} async-done(((bf16[128,2048]{1,0:T(8,128)(2,1)}), bf16[2048,2048]{1,0:T(8,128)(2,1)}) %all-gather.10.cloned.1.call-update) | async-done | bytes 8388624 | tf_op jit(solution)/shard_map/all_gather | solution.py:99
  223.7 5.6 %convolution_convert_fusion = bf16[32,2048]{1,0:T(8,128)(2,1)} fusion(bf16[2048,2048]{1,0:T(8,128)(2,1)} %all-gather.10.cloned.1.call-done, bf16[16,32,128]{2,1,0:T(8,128)(2,1)S(1)} %all_to_all.19), kind=kOutput, calls=%fused_computation | convolution fusion | flops 268500992 | bytes 8650752 | tf_op jit(solution)/shard_map/dot_general | solution.py:97
  (6 shorter events, 0.0 us)
Async XLA Ops:
  6.5 56.2 %all-gather.8.cloned.1.call-start = ((), (), s32[]{:S(2)}) async-start(), calls=%async_computation.2 | async-start | bytes 2228224 | tf_op jit(solution)/shard_map/all_gather | solution.py:33
  7.3 97.7 %all-gather.6.cloned.1.call-start = ((), (), s32[]{:S(2)}) async-start(), calls=%async_computation.1 | async-start | bytes 2228224 | tf_op jit(solution)/shard_map/all_gather | solution.py:29
  8.8 138.5 %all-gather.12.cloned.1.call-start = ((), (), s32[]{:S(2)}) async-start(), calls=%async_computation.4 | async-start | bytes 1183744 | tf_op jit(solution)/shard_map/all_gather | solution.py:15
  14.3 95.9 %copy-start = (bf16[128,128]{1,0:T(8,128)(2,1)S(1)}, bf16[128,128]{1,0:T(8,128)(2,1)}, u32[]{:S(2)}) copy-start(bf16[128,128]{1,0:T(8,128)(2,1)} %param.13) | copy-start | bytes 98308
  110.1 113.6 %all-gather.10.cloned.1.call-start = ((), (), s32[]{:S(2)}) async-start(), calls=%async_computation.3 | async-start | bytes 8912896 | tf_op jit(solution)/shard_map/all_gather | solution.py:99
Sparse Core Ops, SparseCore 0:
  9.8 52.9 all-gather.7
  64.6 40.3 all-gather.5
  110.2 37.0 all-gather.11
  149.6 73.9 all-gather.9
where the time goes:
time: 236 us
  waiting for transfers between devices  166 us (70%)
  blocking collectives  32.2 us (14%)
  between operations  15.9 us (7%)
  matrix products  10.4 us (4%)
  other arithmetic  5.99 us (3%)
  local copies, waits for them, and re-layouts  5.13 us (2%)
    all_gather x1, waiting for transfers between devices, shards(): lax.all_gather(rows_out, 'head', axis=0, tiled=True)  59.6 us
    all_gather x1, waiting for transfers between devices, shards(): lax.all_gather(frames, 'head', axis=0, tiled=True)  48.5 us
    all_gather x1, waiting for transfers between devices, shards(): lax.all_gather(jnp.concatenate([w_query, w_key, w_value, w_gate], axis=1)...  42.3 us
    all_gather x1, blocking collectives, shards(): rows_out = lax.all_gather(w_out, 'tm', axis=1, tiled=True)  19.1 us
    all_gather x1, waiting for transfers between devices, prior_state(): gathered = lax.all_gather(packed, axis)  14.9 us
    all_to_all x1, blocking collectives, shards(): lax.all_to_all(gated, 'head', split_axis=0, concat_axis=1, tiled=True)  13.2 us
    dot_general x1, matrix products, shards(): jnp.dot(owned, lax.all_gather(rows_out, 'head', axis=0, tiled=True), pref...  5.58 us
  transfers between devices with their start and end apart: 4, of which 4 were waited for; matrix products, arithmetic and copies ran while one was open for 5% of the time, Pallas kernels for 0%

commit v1 on v0

--- a/solution.py
+++ b/solution.py
@@ -92,7 +92,9 @@
         .astype(jnp.bfloat16)
         .reshape(local_len, head_width)
     )
-    owned = lax.all_to_all(gated, "head", split_axis=0, concat_axis=1, tiled=True)
+    pieces = jnp.split(gated, lax.axis_size("head"), axis=0)
+    incoming = lax.all_to_all(jnp.stack(pieces), "head", 0, 0)
+    owned = jnp.concatenate(incoming, axis=1)
     rows_out = lax.all_gather(w_out, "tm", axis=1, tiled=True)
     return jnp.dot(
         owned,

time: 236 us -> 236 us (level)
  no operation moved by 1% of the time
where the time goes in v1:
time: 236 us
  waiting for transfers between devices  166 us (70%)
  blocking collectives  32.2 us (14%)
  between operations  16 us (7%)
  matrix products  10.4 us (4%)
  other arithmetic  5.99 us (3%)
  local copies, waits for them, and re-layouts  5.27 us (2%)
    all_gather x1, waiting for transfers between devices, shards(): lax.all_gather(rows_out, 'head', axis=0, tiled=True)  59.4 us
    all_gather x1, waiting for transfers between devices, shards(): lax.all_gather(frames, 'head', axis=0, tiled=True)  48.5 us
    all_gather x1, waiting for transfers between devices, shards(): lax.all_gather(jnp.concatenate([w_query, w_key, w_value, w_gate], axis=1)...  42.3 us
    all_gather x1, blocking collectives, shards(): rows_out = lax.all_gather(w_out, 'tm', axis=1, tiled=True)  19.1 us
    all_gather x1, waiting for transfers between devices, prior_state(): gathered = lax.all_gather(packed, axis)  14.9 us
    all_to_all x1, blocking collectives, shards(): incoming = lax.all_to_all(jnp.stack(pieces), 'head', 0, 0)  13.2 us
    dot_general x1, matrix products, shards(): jnp.dot(owned, lax.all_gather(rows_out, 'head', axis=0, tiled=True), pref...  5.58 us
  transfers between devices with their start and end apart: 4, of which 4 were waited for; matrix products, arithmetic and copies ran while one was open for 5% of the time, Pallas kernels for 0%

profile of v1, /device:TPU:1, one launch (start us, length us, event | category | flops | bytes accessed | tf_op | source)
XLA Modules:
  0.0 235.8 jit_solution(14249617559605364979)
XLA Ops:
  6.5 0.0 all-gather.8.cloned.1.call-start
  6.5 0.7 all-gather.8.cloned.1.call-update
  7.3 0.0 all-gather.6.cloned.1.call-start
  7.3 1.5 pad_maximum_fusion
  8.8 0.0 all-gather.6.cloned.1.call-update
  8.8 0.0 all-gather.12.cloned.1.call-start
  8.9 1.3 reduce_sum.45
  10.2 1.0 reduce-window.6
  11.1 0.7 slice.83
  11.8 0.2 slice_reduce_fusion.1
  12.0 0.2 reduce-window.9
  12.2 0.1 broadcast.153
  12.2 0.6 slice.84
  14.2 0.1 subtract_exponential_fusion
  14.3 0.0 copy-start
  14.3 48.5 %all-gather.8.cloned.1.call-done = bf16[512,2048]{1,0:T(8,128)(2,1)} async-done(((bf16[32,2048]{1,0:T(8,128)(2,1)}), bf16[512,2048]{1,0:T(8,128)(2,1)}) %all-gather.8.cloned.1.call-update) | async-done | bytes 2097168 | tf_op jit(solution)/shard_map/all_gather | solution.py:33
  62.7 42.3 %all-gather.6.cloned.1.call-done = bf16[2048,512]{1,0:T(8,128)(2,1)} async-done(((bf16[128,512]{1,0:T(8,128)(2,1)}), bf16[2048,512]{1,0:T(8,128)(2,1)}) %all-gather.6.cloned.1.call-update) | async-done | bytes 2097168 | tf_op jit(solution)/shard_map/all_gather | solution.py:29
  105.0 3.5 %fusion.35 = (bf16[512,512]{1,0:T(8,128)(2,1)S(1)}, f32[512,512]{1,0:T(8,128)S(1)}) fusion(bf16[512,2048]{1,0:T(8,128)(2,1)} %all-gather.8.cloned.1.call-done, bf16[2048,512]{1,0:T(8,128)(2,1)} %all-gather.6.cloned.1.call-done), kind=kOutput, calls=%fused_computation.87 | convolution fusion | flops 1074003968 | bytes 5767168 | tf_op jit(solution)/shard_map/dot_general | solution.py:32
  108.5 0.3 fusion.4
  108.8 1.3 concatenate.7
  110.1 0.0 all-gather.12.cloned.1.call-update
  110.1 0.0 all-gather.10.cloned.1.call-start
  110.1 0.0 copy-done
  110.1 19.1 %all_gather.22 = bf16[128,2048]{1,0:T(8,128)(2,1)} all-gather(bf16[128,128]{1,0:T(8,128)(2,1)S(1)} %copy-done), channel_id=1, replica_groups=mesh['tm'=16,'head'=16] {'tm'}, dimensions={1}, use_global_device_ids=true | all-gather | bytes 557056 | tf_op jit(solution)/shard_map/all_gather | solution.py:98
  129.2 0.0 all-gather.10.cloned.1.call-update
  129.2 0.6 slice.81
  129.9 0.6 slice.82
  131.9 0.5 fusion.2
  132.4 14.9 %all-gather.12.cloned.1.call-done = f32[16,136,128]{2,1,0:T(8,128)} async-done(((f32[1,136,128]{2,1,0:T(8,128)}), f32[16,136,128]{2,1,0:T(8,128)}) %all-gather.12.cloned.1.call-update) | async-done | bytes 1114128 | tf_op jit(solution)/shard_map/all_gather | solution.py:15
  147.3 1.0 slice_reduce_fusion
  148.4 0.1 select_reduce_fusion
  148.5 1.4 fusion.5
  149.9 0.5 fusion.36
  150.4 0.2 fusion.13
  150.7 0.2 fusion.16
  151.1 13.2 %all_to_all.5 = bf16[16,32,128]{2,1,0:T(8,128)(2,1)S(1)} all-to-all(bf16[16,32,128]{2,1,0:T(8,128)(2,1)S(1)} %constant_dynamic-update-slice_fusion), channel_id=1, replica_groups=mesh['tm'=16,'head'=16] {'head'}, dimensions={0} | all-to-all | bytes 262144 | tf_op jit(solution)/shard_map/all_to_all | solution.py:96
  164.2 59.4 %all-gather.10.cloned.1.call-done = bf16[2048,2048]{1,0:T(8,128)(2,1)} async-done(((bf16[128,2048]{1,0:T(8,128)(2,1)}), bf16[2048,2048]{1,0:T(8,128)(2,1)}) %all-gather.10.cloned.1.call-update) | async-done | bytes 8388624 | tf_op jit(solution)/shard_map/all_gather | solution.py:101
  223.7 5.6 %convolution_convert_fusion = bf16[32,2048]{1,0:T(8,128)(2,1)} fusion(bf16[2048,2048]{1,0:T(8,128)(2,1)} %all-gather.10.cloned.1.call-done, bf16[16,32,128]{2,1,0:T(8,128)(2,1)S(1)} %all_to_all.5), kind=kOutput, calls=%fused_computation | convolution fusion | flops 268500992 | bytes 8650752 | tf_op jit(solution)/shard_map/dot_general | solution.py:99
  (22 shorter events, 0.2 us)
Async XLA Ops:
  6.5 56.2 %all-gather.8.cloned.1.call-start = ((), (), s32[]{:S(2)}) async-start(), calls=%async_computation.2 | async-start | bytes 2228224 | tf_op jit(solution)/shard_map/all_gather | solution.py:33
  7.3 97.7 %all-gather.6.cloned.1.call-start = ((), (), s32[]{:S(2)}) async-start(), calls=%async_computation.1 | async-start | bytes 2228224 | tf_op jit(solution)/shard_map/all_gather | solution.py:29
  8.8 138.5 %all-gather.12.cloned.1.call-start = ((), (), s32[]{:S(2)}) async-start(), calls=%async_computation.4 | async-start | bytes 1183744 | tf_op jit(solution)/shard_map/all_gather | solution.py:15
  14.3 95.9 %copy-start = (bf16[128,128]{1,0:T(8,128)(2,1)S(1)}, bf16[128,128]{1,0:T(8,128)(2,1)}, u32[]{:S(2)}) copy-start(bf16[128,128]{1,0:T(8,128)(2,1)} %param.13) | copy-start | bytes 98308
  110.1 113.6 %all-gather.10.cloned.1.call-start = ((), (), s32[]{:S(2)}) async-start(), calls=%async_computation.3 | async-start | bytes 8912896 | tf_op jit(solution)/shard_map/all_gather | solution.py:101
Sparse Core Ops, SparseCore 0:
  9.8 52.9 all-gather.7
  64.6 40.3 all-gather.5
  110.2 37.0 all-gather.11
  149.6 73.9 all-gather.9
